TPU v7x, 256 devices: a whole 4x4x8 slice. The times are simulated.
256 devices in a mesh: ctx: 8 (over x, z_lo), tp: 32 (over z_hi, y, core).
Axes of the slice: x: 4, y: 4, z: 8 (z_hi: 4, z_lo: 2; z = z_hi * 2 + z_lo), core: 2. Of those that a mesh axis runs over, the one named last changes fastest.
Arguments:
- states: bfloat16 [8192, 2048], P(('ctx', 'tp')), may hold values from -6 to 6
- short_lengths: int32 [64], P('ctx'), may hold values from 1 to 64, 3072 in all
- attn_gain: float32 [2048], replicated, may hold values from 0.5 to 16
- wq: bfloat16 [2048, 2048], P(None, 'tp'), may hold values from -0.125 to 0.125
- wkv: bfloat16 [2048, 512], replicated, may hold values from -0.125 to 0.125
- wo: bfloat16 [2048, 2048], P('tp'), may hold values from -0.125 to 0.125
- mlp_gain: float32 [2048], replicated, may hold values from 0.5 to 1.5
- w_gate: bfloat16 [2048, 5632], P(None, 'tp'), may hold values from -0.125 to 0.125
- w_up: bfloat16 [2048, 5632], P(None, 'tp'), may hold values from -0.125 to 0.125
- w_down: bfloat16 [5632, 2048], P('tp'), may hold values from -0.078125 to 0.078125
Outputs:
- updated: bfloat16 [8192, 2048], P(('ctx', 'tp'))
- long_cache: bfloat16 [2, 2048, 512], P(None, 'ctx', 'tp')
- short_cache: bfloat16 [64, 64, 512], P('ctx', None, 'tp')
Inputs may be any that keep to these rules, and one draw needn't show every extreme that they name: `short_lengths`: rows of a short prompt at or beyond its length are padding; the largest length is 64.
All inputs are finite; a program needn't handle non-finite values. No bound on the sum of `short_lengths` on one device may be relied on, other than what follows from the above.
Results may differ from a plain program's by a relative error of at most 0.022.
The roundings to bfloat16 on the way count: a program that leaves them out, or rounds other values in their place, can miss the bound.
Values may be sent and summed in bfloat16 or wider, within the bound.
No kernel may reach another device: no remote copies, remote signals or barrier semaphores. Data moves between devices by JAX's collectives and lax.ppermute only.
A program may use at most 64 MiB of HBM per device.

v0:
```python
import jax
import jax.numpy as jnp
from jax import lax
from jax.sharding import PartitionSpec as P

KVH = 4
HEAD_SIZE = 64
LONG = 2
LLEN = 2048
SLEN = 64
EPS = 1e-05
THETA = 10000.0
NEG = -1e30


def rms_scale(matrix, gain):
    entries = matrix.astype(jnp.float32)
    power = jnp.mean(entries * entries, axis=-1, keepdims=True)
    return (entries * lax.rsqrt(power + EPS) * gain).astype(jnp.bfloat16)


def rotate(entries, positions):
    half_width = entries.shape[-1] // 2
    frequency = THETA ** (-jnp.arange(half_width, dtype=jnp.float32) * 2.0 / entries.shape[-1])
    angles = positions.astype(jnp.float32)[:, None] * frequency[None, :]
    cosine = jnp.cos(angles)[:, None, :]
    sine_wave = jnp.sin(angles)[:, None, :]
    first_half = entries[..., :half_width]
    second_half = entries[..., half_width:]
    return jnp.concatenate(
        [
            first_half * cosine - second_half * sine_wave,
            second_half * cosine + first_half * sine_wave,
        ],
        axis=-1,
    )


def rank_positions(ctx_rank, rank_rows, block_len, long_rows, n_blocks):
    index_row = jnp.arange(rank_rows, dtype=jnp.int32)
    half_index = index_row // block_len % 2
    offset_row = index_row % block_len
    which_block = jnp.where(half_index == 0, ctx_rank, n_blocks - 1 - ctx_rank)
    long_pos = which_block * block_len + offset_row
    short_pos = (index_row - long_rows) % SLEN
    return jnp.where(index_row < long_rows, long_pos, short_pos)


def project(matrix, positions, wq, wkv_head, heads_dev):
    row_count = matrix.shape[0]
    query_matrix = jnp.dot(matrix, wq, preferred_element_type=jnp.float32).reshape(
        row_count, heads_dev, HEAD_SIZE
    )
    query_matrix = rotate(query_matrix, positions).astype(jnp.bfloat16)
    pairs = jnp.dot(matrix, wkv_head, preferred_element_type=jnp.float32)
    key_matrix = rotate(pairs[:, None, :HEAD_SIZE], positions).astype(jnp.bfloat16)[:, 0]
    value_matrix = pairs[:, HEAD_SIZE:].astype(jnp.bfloat16)
    return jnp.concatenate(
        [query_matrix.reshape(row_count, heads_dev * HEAD_SIZE), key_matrix, value_matrix], axis=1
    )


def attend(soft_state, query_matrix, query_pos, key_matrix, value_matrix, key_pos, valid_keys):
    best_score, weight_sum, weighted = soft_state
    logit_scores = jnp.einsum(
        "rzsm,rvm->rzsv", query_matrix, key_matrix, preferred_element_type=jnp.float32
    ) * HEAD_SIZE ** (-0.5)
    allowed = (key_pos[None, :] <= query_pos[:, None])[None, None] & valid_keys[:, None, None, :]
    logit_scores = jnp.where(allowed, logit_scores, NEG)
    new_best = jnp.maximum(best_score, jnp.max(logit_scores, axis=-1))
    weights = jnp.where(allowed, jnp.exp(logit_scores - new_best[..., None]), 0.0)
    weight_sum = jnp.sum(weights, axis=-1)
    weighted = jnp.einsum(
        "awlp,ape->awle",
        weights.astype(jnp.bfloat16),
        value_matrix,
        preferred_element_type=jnp.float32,
    )
    return (new_best, weight_sum, weighted)


def per_device(states, short_lengths, attn_gain, wq, wkv, wo, mlp_gain, w_gate, w_up, w_down):
    n_ctx = lax.axis_size("ctx")
    n_tp = lax.axis_size("tp")
    ctx_rank = lax.axis_index("ctx")
    tp_index = lax.axis_index("tp")
    tok_rows = states.shape[0]
    rank_rows = tok_rows * n_tp
    n_blocks = 2 * n_ctx
    block_len = LLEN // n_blocks
    long_rows = LONG * 2 * block_len
    heads_dev = wq.shape[1] // HEAD_SIZE
    q_cols = heads_dev * HEAD_SIZE
    pair_width = 2 * HEAD_SIZE
    cache_cols = KVH * pair_width // n_tp
    kv_group = tp_index * KVH // n_tp
    wkv_head = lax.dynamic_slice_in_dim(wkv, kv_group * pair_width, pair_width, 1)
    first_col = tp_index * cache_cols - kv_group * pair_width
    positions = rank_positions(ctx_rank, rank_rows, block_len, long_rows, n_blocks)
    packed = project(
        lax.all_gather(rms_scale(states, attn_gain), "tp", axis=0, tiled=True),
        positions,
        wq,
        wkv_head,
        heads_dev,
    )
    query_matrix = packed[:, :q_cols].reshape(rank_rows, heads_dev, HEAD_SIZE)
    key_matrix = packed[:, q_cols : q_cols + HEAD_SIZE]
    value_matrix = packed[:, q_cols + HEAD_SIZE :]
    long_q = (
        query_matrix[:long_rows]
        .reshape(LONG, 2 * block_len, heads_dev, HEAD_SIZE)
        .transpose(0, 2, 1, 3)
    )
    long_k = key_matrix[:long_rows].reshape(LONG, 2, 1, block_len, HEAD_SIZE)
    long_v = value_matrix[:long_rows].reshape(LONG, 2, 1, block_len, HEAD_SIZE)
    long_qpos = positions[: 2 * block_len]
    half_pick = jnp.arange(2, dtype=jnp.int32)[:, None, None]
    long_init = (
        jnp.full((LONG, heads_dev, 2 * block_len), NEG, jnp.float32),
        jnp.zeros((LONG, heads_dev, 2 * block_len), jnp.float32),
        jnp.zeros((LONG, heads_dev, 2 * block_len, HEAD_SIZE), jnp.float32),
        jnp.zeros((LONG, 2, block_len, cache_cols), jnp.float32),
    )
    gathered = lax.all_gather(jnp.stack([long_k[:, :, 0], long_v[:, :, 0]]), "ctx", axis=0)
    piece_k = jnp.moveaxis(gathered[:, 0], 0, 2)
    piece_v = jnp.moveaxis(gathered[:, 1], 0, 2)
    piece_blocks = piece_k.shape[2]
    block_ids = jnp.arange(piece_blocks, dtype=jnp.int32)
    held_blocks = jnp.stack([block_ids, n_blocks - 1 - block_ids])
    key_pos = (
        held_blocks[:, :, None] * block_len + jnp.arange(block_len, dtype=jnp.int32)
    ).reshape(-1)
    key_count = 2 * piece_blocks * block_len
    flat_k = piece_k.reshape(LONG, key_count, HEAD_SIZE)
    flat_v = piece_v.reshape(LONG, key_count, HEAD_SIZE)
    all_valid = jnp.ones((LONG, key_count), dtype=bool)
    soft_state = long_init[:3]
    soft_state = attend(soft_state, long_q, long_qpos, flat_k, flat_v, key_pos, all_valid)
    joined = jnp.concatenate([piece_k, piece_v], axis=-1)
    own_cols = lax.dynamic_slice_in_dim(joined, first_col, cache_cols, 4)
    selector = ((held_blocks[None] // 2 == ctx_rank) & (held_blocks[None] % 2 == half_pick)).astype(
        jnp.bfloat16
    )
    cache_rows = jnp.einsum(
        "ehj,phjbc->pebc", selector, own_cols, preferred_element_type=jnp.float32
    )
    folded = soft_state + (cache_rows,)
    long_out = (
        (folded[2] / folded[1][..., None])
        .astype(jnp.bfloat16)
        .transpose(0, 2, 1, 3)
        .reshape(long_rows, q_cols)
    )
    long_cache = folded[3].astype(jnp.bfloat16).reshape(LONG, 2 * block_len, cache_cols)
    short_count = short_lengths.shape[0]
    short_q = (
        query_matrix[long_rows:]
        .reshape(short_count, SLEN, heads_dev, HEAD_SIZE)
        .transpose(0, 2, 1, 3)
    )
    short_k = key_matrix[long_rows:].reshape(short_count, SLEN, HEAD_SIZE)
    short_v = value_matrix[long_rows:].reshape(short_count, SLEN, HEAD_SIZE)
    offsets = jnp.arange(SLEN, dtype=jnp.int32)
    short_valid = offsets[None, :] < short_lengths[:, None]
    short_init = (
        jnp.full((short_count, heads_dev, SLEN), NEG, jnp.float32),
        jnp.zeros((short_count, heads_dev, SLEN), jnp.float32),
        jnp.zeros((short_count, heads_dev, SLEN, HEAD_SIZE), jnp.float32),
    )
    short_state = attend(short_init, short_q, offsets, short_k, short_v, offsets, short_valid)
    short_out = (
        (short_state[2] / short_state[1][..., None])
        .astype(jnp.bfloat16)
        .transpose(0, 2, 1, 3)
        .reshape(short_count * SLEN, q_cols)
    )
    short_cache = lax.dynamic_slice_in_dim(
        jnp.concatenate([short_k, short_v], axis=-1), first_col, cache_cols, 2
    )
    attn = jnp.concatenate([long_out, short_out], axis=0)
    mixed = lax.psum_scatter(
        jnp.dot(attn, wo, preferred_element_type=jnp.float32).astype(jnp.bfloat16),
        "tp",
        scatter_dimension=0,
        tiled=True,
    ).astype(jnp.float32)
    residual = (states.astype(jnp.float32) + mixed).astype(jnp.bfloat16)
    piece = lax.all_gather(rms_scale(residual, mlp_gain), "tp", axis=0, tiled=True)
    gate = jnp.dot(piece, w_gate, preferred_element_type=jnp.float32)
    up_part = jnp.dot(piece, w_up, preferred_element_type=jnp.float32)
    hidden = (jax.nn.silu(gate) * up_part).astype(jnp.bfloat16)
    down = lax.psum_scatter(
        jnp.dot(hidden, w_down, preferred_element_type=jnp.float32).astype(jnp.bfloat16),
        "tp",
        scatter_dimension=0,
        tiled=True,
    ).astype(jnp.float32)
    updated = (residual.astype(jnp.float32) + down).astype(jnp.bfloat16)
    return (updated, long_cache, short_cache)


def solution(mesh):
    in_specs = (
        P(("ctx", "tp"), None),
        P("ctx"),
        P(),
        P(None, "tp"),
        P(),
        P("tp", None),
        P(),
        P(None, "tp"),
        P(None, "tp"),
        P("tp", None),
    )
    out_specs = (P(("ctx", "tp"), None), P(None, "ctx", "tp"), P("ctx", None, "tp"))
    return jax.shard_map(
        per_device, mesh=mesh, in_specs=in_specs, out_specs=out_specs, check_vma=False
    )
```

profile of v0, /device:TPU:2, one launch (start us, length us, event | category | flops | bytes accessed | tf_op | source)
XLA Modules:
  0.0 415.9 jit_solution(9527063426652451580)
XLA Ops:
  7.2 0.0 copy-start
  7.2 0.0 all-gather.5.cloned.1.call-start
  7.2 1.2 fusion.28
  8.4 1.7 fusion.30
  10.1 0.0 all-gather.5.cloned.1.call-update
  10.1 0.0 all-gather.9.cloned.1.call-start
  10.2 0.0 copy-start.9
  10.3 0.0 copy-start.6
  10.3 64.2 %all-gather.5.cloned.1.call-done = bf16[1024,2048]{1,0:T(8,128)(2,1)} async-done(((bf16[32,2048]{1,0:T(8,128)(2,1)}), bf16[1024,2048]{1,0:T(8,128)(2,1)}) %all-gather.5.cloned.1.call-update) | async-done | bytes 4194320 | tf_op jit(solution)/shard_map/all_gather | solution.py:101
  74.5 0.0 copy-done
  74.5 3.7 fusion.106
  78.2 0.0 copy-done.9
  78.2 0.0 copy-start.12
  78.2 0.0 slice-start
  78.3 3.6 convolution_bitcast_fusion
  81.9 0.6 fusion.52
  82.6 0.7 pad_maximum_fusion
  83.2 0.0 all-gather.9.cloned.1.call-update
  83.3 0.0 reduce-scatter.3.cloned.1.call-start
  83.3 0.0 copy-start.10
  83.4 0.1 iota_compare_fusion.1
  83.4 0.4 copy-done.10
  83.8 0.1 add_bitcast_fusion
  83.9 1.2 broadcast_compare_fusion
  85.1 0.1 reshape.510
  85.3 0.1 reshape.509
  85.4 0.0 copy-start.5
  85.4 0.1 copy.49
  85.5 0.3 fusion.105
  85.8 0.1 fusion.36
  86.0 0.5 fusion.8
  86.4 0.1 copy.43
  86.5 36.2 %all-gather.9.cloned.1.call-done = bf16[16,2,2,128,64]{3,4,2,1,0:T(8,128)(2,1)} async-done(((bf16[2,2,2,128,64]{3,4,2,1,0:T(8,128)(2,1)}), bf16[16,2,2,128,64]{3,4,2,1,0:T(8,128)(2,1)}) %all-gather.9.cloned.1.call-update) | async-done | bytes 1048592 | tf_op jit(solution)/shard_map/all_gather | solution.py:125
  122.7 2.1 fusion.103
  124.8 0.3 copy.66
  125.2 1.0 reshape.506
  126.2 1.4 copy.65
  127.6 1.0 reshape.507
  128.6 2.4 fusion
  131.0 1.4 fusion.1
  132.4 0.0 copy-start.7
  132.4 1.1 fusion.17
  133.6 0.0 copy-start.2
  133.6 0.0 copy-start.8
  133.6 3.2 convolution_convert_fusion.1
  136.8 0.0 reduce-scatter.3.cloned.1.call-update
  136.9 0.0 all-gather.7.cloned.1.call-start
  136.9 100.0 %reduce-scatter.3.cloned.1.call-done = bf16[32,2048]{1,0:T(8,128)(2,1)} async-done(((bf16[1024,2048]{1,0:T(8,128)(2,1)}), bf16[32,2048]{1,0:T(8,128)(2,1)}) %reduce-scatter.3.cloned.1.call-update) | async-done | bytes 131088 | tf_op jit(solution)/shard_map/reduce_scatter | solution.py:182
  236.9 0.0 copy-done.2
  236.9 1.1 fusion.32
  238.0 1.7 fusion.34
  239.7 0.0 all-gather.7.cloned.1.call-update
  239.7 0.2 reduce-scatter.5.cloned.1.call-start
  239.9 57.9 %all-gather.7.cloned.1.call-done = bf16[1024,2048]{1,0:T(8,128)(2,1)} async-done(((bf16[32,2048]{1,0:T(8,128)(2,1)}), bf16[1024,2048]{1,0:T(8,128)(2,1)}) %all-gather.7.cloned.1.call-update) | async-done | bytes 4194320 | tf_op jit(solution)/shard_map/all_gather | solution.py:189
  297.9 4.8 %fusion.107 = f32[1024,176]{0,1:T(8,128)} fusion(bf16[1024,2048]{1,0:T(8,128)(2,1)} %all-gather.7.cloned.1.call-done, bf16[2048,176]{0,1:T(8,128)(2,1)} %param.17), kind=kOutput, calls=%fused_computation.160 | convolution fusion | flops 738197504 | bytes 5636096 | tf_op jit(solution)/shard_map/dot_general | solution.py:190
  302.7 7.5 %convolution_convert_fusion = bf16[1024,2048]{1,0:T(8,128)(2,1)} fusion(bf16[176,2048]{1,0:T(8,128)(2,1)} %param.19, bf16[1024,2048]{1,0:T(8,128)(2,1)} %all-gather.7.cloned.1.call-done, bf16[2048,176]{0,1:T(8,128)(2,1)} %param.18, f32[1024,176]{0,1:T(8,128)} %fusion.107), kind=kOutput, calls=%fused_computation.2 | convolution fusion | flops 1479573504 | bytes 10551296 | tf_op jit(solution)/shard_map/dot_general | solution.py:194
  310.2 0.0 reduce-scatter.5.cloned.1.call-update
  310.2 0.6 copy-done.11
  310.9 0.9 copy.44
  311.8 0.7 fusion.68
  312.5 0.3 fusion.10
  312.7 0.6 reshape.511
  313.3 94.4 %reduce-scatter.5.cloned.1.call-done = bf16[32,2048]{1,0:T(8,128)(2,1)} async-done(((bf16[1024,2048]{1,0:T(8,128)(2,1)}), bf16[32,2048]{1,0:T(8,128)(2,1)}) %reduce-scatter.5.cloned.1.call-update) | async-done | bytes 131088 | tf_op jit(solution)/shard_map/reduce_scatter | solution.py:193
  407.8 1.6 fusion.35
  (35 shorter events, 0.3 us)
Async XLA Ops:
  7.2 67.3 %copy-start = (bf16[2048,512]{1,0:T(8,128)(2,1)S(1)}, bf16[2048,512]{1,0:T(8,128)(2,1)}, u32[]{:S(2)}) copy-start(bf16[2048,512]{1,0:T(8,128)(2,1)} %param.14) | copy-start | bytes 6291460
  7.2 67.3 %all-gather.5.cloned.1.call-start = ((), (), s32[]{:S(2)}) async-start(), calls=%async_computation.2 | async-start | bytes 4325376 | tf_op jit(solution)/shard_map/all_gather | solution.py:101
  10.1 112.6 %all-gather.9.cloned.1.call-start = ((), (), s32[]{:S(2)}) async-start(), calls=%async_computation.6 | async-start | bytes 1179648 | tf_op jit(solution)/shard_map/all_gather | solution.py:125
  10.2 68.0 %copy-start.9 = (s32[1024]{0:T(1024)}, s32[1024]{0:T(1024)S(1)}, u32[]{:S(2)}) copy-start(s32[1024]{0:T(1024)S(1)} %fusion.78) | copy-start | bytes 12292
  10.3 68.0 %copy-start.6 = (bf16[2048,64]{0,1:T(8,128)(2,1)S(1)}, bf16[2048,64]{0,1:T(8,128)(2,1)}, u32[]{:S(2)}) copy-start(bf16[2048,64]{0,1:T(8,128)(2,1)} %param.13) | copy-start | bytes 786436
  78.2 5.1 %copy-start.12 = (s32[8]{0:T(128)S(1)}, s32[8]{0:T(128)}, u32[]{:S(2)}) copy-start(s32[8]{0:T(128)} %param.11) | copy-start | bytes 100
  78.2 5.7 %slice-start = ((s32[1024]{0:T(1024)}), s32[256]{0:T(256)S(1)}, s32[]{:S(2)}) async-start(s32[1024]{0:T(1024)} %copy-done.9), calls=%async_computation.7 | async-start | bytes 2048 | tf_op jit(solution)/shard_map/slice | solution.py:117
  83.3 153.7 %reduce-scatter.3.cloned.1.call-start = ((), (), s32[]{:S(2)}) async-start(), calls=%async_computation.3 | async-start | bytes 4325376 | tf_op jit(solution)/shard_map/reduce_scatter | solution.py:182
  83.3 0.5 copy-start.10
  85.4 39.4 %copy-start.5 = (bf16[8,64,64]{1,0,2:T(8,128)(2,1)}, bf16[8,64,64]{1,0,2:T(8,128)(2,1)S(1)}, u32[]{:S(2)}) copy-start(bf16[8,64,64]{1,0,2:T(8,128)(2,1)S(1)} %reshape.509) | copy-start | bytes 196612
  128.6 2.4 copy-start.1
  128.6 3.8 copy-start.4
  132.4 1.2 copy-start.7
  133.6 103.4 %copy-start.2 = (bf16[32,2048]{1,0:T(8,128)(2,1)S(1)}, bf16[32,2048]{1,0:T(8,128)(2,1)}, u32[]{:S(2)}) copy-start(bf16[32,2048]{1,0:T(8,128)(2,1)} %param.10) | copy-start | bytes 393220
  133.6 104.4 %copy-start.8 = (f32[2048]{0:T(1024)S(1)}, f32[2048]{0:T(1024)}, u32[]{:S(2)}) copy-start(f32[2048]{0:T(1024)} %param.16) | copy-start | bytes 24580
  136.9 161.0 %all-gather.7.cloned.1.call-start = ((), (), s32[]{:S(2)}) async-start(), calls=%async_computation.4 | async-start | bytes 4325376 | tf_op jit(solution)/shard_map/all_gather | solution.py:189
  239.7 168.1 %reduce-scatter.5.cloned.1.call-start = ((), (), s32[]{:S(2)}) async-start(), calls=%async_computation.5 | async-start | bytes 4325376 | tf_op jit(solution)/shard_map/reduce_scatter | solution.py:193
  310.2 0.7 copy-start.11
  310.2 97.6 %copy-start.3 = (bf16[32,2048]{1,0:T(8,128)(2,1)S(1)}, bf16[32,2048]{1,0:T(8,128)(2,1)}, u32[]{:S(2)}) copy-start(bf16[32,2048]{1,0:T(8,128)(2,1)} %reduce-scatter.3.cloned.1.call-done) | copy-start | bytes 393220
Sparse Core Ops, SparseCore 0:
  11.1 63.2 all-gather.4
  83.4 39.3 all-gather.8
  137.0 99.9 reduce-scatter.2
  240.2 57.5 all-gather.6
  310.3 97.3 reduce-scatter.4
where the time goes:
time: 416 us
  waiting for transfers between devices  353 us (85%)
  matrix products  27.3 us (7%)
  between operations  14.1 us (3%)
  other arithmetic  12.1 us (3%)
  local copies, waits for them, and re-layouts  9.11 us (2%)
    reduce_scatter x1, waiting for transfers between devices, per_device(): lax.psum_scatter(jnp.dot(attn, wo, preferred_element_type=jnp.float32).as...  100 us
    reduce_scatter x1, waiting for transfers between devices, per_device(): lax.psum_scatter(jnp.dot(hidden, w_down, preferred_element_type=jnp.float...  94.4 us
    all_gather x1, waiting for transfers between devices, per_device(): lax.all_gather(rms_scale(states, attn_gain), 'tp', axis=0, tiled=True)  64.2 us
    all_gather x1, waiting for transfers between devices, per_device(): lax.all_gather(rms_scale(residual, mlp_gain), 'tp', axis=0, tiled=True)  57.9 us
    all_gather x1, waiting for transfers between devices, per_device(): lax.all_gather(jnp.stack([long_k[:, :, 0], long_v[:, :, 0]]), 'ctx', axis=0)  36.2 us
  transfers between devices with their start and end apart: 5, of which 5 were waited for; matrix products, arithmetic and copies ran while one was open for 1% of the time, Pallas kernels for 0%

commit v1 on v0

--- a/solution.py
+++ b/solution.py
@@ -186,7 +186,12 @@
         tiled=True,
     ).astype(jnp.float32)
     residual = (states.astype(jnp.float32) + mixed).astype(jnp.bfloat16)
-    piece = lax.all_gather(rms_scale(residual, mlp_gain), "tp", axis=0, tiled=True)
+    piece = jnp.concatenate(
+        lax.all_to_all(
+            jnp.stack([rms_scale(residual, mlp_gain)] * lax.axis_size("tp"), axis=0), "tp", 0, 0
+        ),
+        axis=0,
+    )
     gate = jnp.dot(piece, w_gate, preferred_element_type=jnp.float32)
     up_part = jnp.dot(piece, w_up, preferred_element_type=jnp.float32)
     hidden = (jax.nn.silu(gate) * up_part).astype(jnp.bfloat16)

time: 416 us -> 459 us (1.10)
  blocking collectives: 0 us -> 101 us
  waiting for transfers between devices: 353 us -> 295 us
    all_to_all x0 -> x1, blocking collectives: none -> 101 us  [per_device(): lax.all_to_all(jnp.stack([rms_scale(residual, mlp_gain)] * lax.axis_size(...]
    all_gather x1 -> x0, waiting for transfers between devices: 57.9 us -> none  [per_device(): lax.all_gather(rms_scale(residual, mlp_gain), 'tp', axis=0, tiled=True)]
  transfers between devices with their start and end apart: 5 -> 4, of which waited for: 5 -> 4; matrix products, arithmetic and copies ran while one was open for 1% -> 1% of each run, Pallas kernels for 0% -> 0%
where the time goes in v1:
time: 459 us
  waiting for transfers between devices  295 us (64%)
  blocking collectives  101 us (22%)
  matrix products  24.9 us (5%)
  between operations  14.2 us (3%)
  local copies, waits for them, and re-layouts  11.6 us (3%)
  other arithmetic  11.4 us (2%)
    all_to_all x1, blocking collectives, per_device(): lax.all_to_all(jnp.stack([rms_scale(residual, mlp_gain)] * lax.axis_size(...  101 us
    reduce_scatter x1, waiting for transfers between devices, per_device(): lax.psum_scatter(jnp.dot(attn, wo, preferred_element_type=jnp.float32).as...  100 us
    reduce_scatter x1, waiting for transfers between devices, per_device(): lax.psum_scatter(jnp.dot(hidden, w_down, preferred_element_type=jnp.float...  94.8 us
    all_gather x1, waiting for transfers between devices, per_device(): lax.all_gather(rms_scale(states, attn_gain), 'tp', axis=0, tiled=True)  64.2 us
    all_gather x1, waiting for transfers between devices, per_device(): lax.all_gather(jnp.stack([long_k[:, :, 0], long_v[:, :, 0]]), 'ctx', axis=0)  36.2 us
  transfers between devices with their start and end apart: 4, of which 4 were waited for; matrix products, arithmetic and copies ran while one was open for 1% of the time, Pallas kernels for 0%

profile of v1, /device:TPU:2, one launch (start us, length us, event | category | flops | bytes accessed | tf_op | source)
XLA Modules:
  0.0 458.7 jit_solution(1070852615516728946)
XLA Ops:
  7.2 0.0 copy-start
  7.2 0.0 all-gather.4.cloned.1.call-start
  7.2 1.2 fusion.28
  8.4 1.7 fusion.30
  10.1 0.0 all-gather.4.cloned.1.call-update
  10.1 0.0 all-gather.6.cloned.1.call-start
  10.2 0.0 copy-start.10
  10.3 0.0 copy-start.7
  10.3 64.2 %all-gather.4.cloned.1.call-done = bf16[1024,2048]{1,0:T(8,128)(2,1)} async-done(((bf16[32,2048]{1,0:T(8,128)(2,1)}), bf16[1024,2048]{1,0:T(8,128)(2,1)}) %all-gather.4.cloned.1.call-update) | async-done | bytes 4194320 | tf_op jit(solution)/shard_map/all_gather | solution.py:101
  74.5 0.0 copy-done
  74.5 3.7 fusion.106
  78.2 0.0 copy-start.14
  78.2 0.0 slice-start
  78.3 3.6 convolution_bitcast_fusion
  81.9 0.6 fusion.52
  82.6 0.7 pad_maximum_fusion
  83.2 0.0 all-gather.6.cloned.1.call-update
  83.3 0.0 reduce-scatter.3.cloned.1.call-start
  83.3 0.0 copy-start.11
  83.4 0.1 iota_compare_fusion.1
  83.4 0.4 copy-done.11
  83.8 0.1 add_bitcast_fusion
  83.9 1.2 broadcast_compare_fusion
  85.1 0.1 reshape.515
  85.3 0.1 reshape.514
  85.4 0.1 copy.49
  85.5 0.3 fusion.105
  85.8 0.1 fusion.36
  86.0 0.5 fusion.8
  86.4 0.1 copy.43
  86.5 36.2 %all-gather.6.cloned.1.call-done = bf16[16,2,2,128,64]{3,4,2,1,0:T(8,128)(2,1)} async-done(((bf16[2,2,2,128,64]{3,4,2,1,0:T(8,128)(2,1)}), bf16[16,2,2,128,64]{3,4,2,1,0:T(8,128)(2,1)}) %all-gather.6.cloned.1.call-update) | async-done | bytes 1048592 | tf_op jit(solution)/shard_map/all_gather | solution.py:125
  122.7 2.1 fusion.103
  124.8 0.3 copy.66
  125.2 1.0 reshape.511
  126.2 1.4 copy.65
  127.6 1.0 reshape.512
  128.6 2.4 fusion
  131.0 1.4 fusion.1
  132.4 0.0 copy-start.8
  132.4 1.1 fusion.17
  133.6 0.0 copy-done.8
  133.6 0.0 copy-start.3
  133.6 0.0 copy-start.9
  133.6 3.2 convolution_convert_fusion.1
  136.8 0.0 reduce-scatter.3.cloned.1.call-update
  136.9 0.0 reduce-scatter.5.cloned.1.call-start
  136.9 100.1 %reduce-scatter.3.cloned.1.call-done = bf16[32,2048]{1,0:T(8,128)(2,1)} async-done(((bf16[1024,2048]{1,0:T(8,128)(2,1)}), bf16[32,2048]{1,0:T(8,128)(2,1)}) %reduce-scatter.3.cloned.1.call-update) | async-done | bytes 131088 | tf_op jit(solution)/shard_map/reduce_scatter | solution.py:182
  237.0 1.1 fusion.32
  238.1 1.0 fusion.34
  239.1 0.5 stack.8
  239.6 0.0 copy-start.13
  239.6 101.1 %all_to_all.5 = bf16[32,32,2048]{2,1,0:T(8,128)(2,1)S(1)} all-to-all(bf16[32,32,2048]{2,1,0:T(8,128)(2,1)S(1)} %stack.8), channel_id=1, replica_groups=mesh['ctx'=8,'tp'=32] {'tp'}, dimensions={0} | all-to-all | bytes 8388608 | tf_op jit(solution)/shard_map/all_to_all | solution.py:190
  340.7 2.0 copy-done.2
  342.7 2.5 fusion.107
  345.2 7.5 %convolution_convert_fusion = bf16[1024,2048]{1,0:T(8,128)(2,1)} fusion(bf16[176,2048]{1,0:T(8,128)(2,1)} %param.19, bf16[1024,2048]{1,0:T(8,128)(2,1)} %bitcast.74, bf16[2048,176]{0,1:T(8,128)(2,1)} %param.18, f32[1024,176]{0,1:T(8,128)} %fusion.107), kind=kOutput, calls=%fused_computation.2 | convolution fusion | flops 1479573504 | bytes 10551296 | tf_op jit(solution)/shard_map/dot_general | solution.py:199
  352.6 0.0 reduce-scatter.5.cloned.1.call-update
  352.7 0.6 copy-done.12
  353.3 0.9 copy.44
  354.3 0.7 fusion.68
  354.9 0.3 fusion.10
  355.2 0.6 reshape.517
  355.8 94.8 %reduce-scatter.5.cloned.1.call-done = bf16[32,2048]{1,0:T(8,128)(2,1)} async-done(((bf16[1024,2048]{1,0:T(8,128)(2,1)}), bf16[32,2048]{1,0:T(8,128)(2,1)}) %reduce-scatter.5.cloned.1.call-update) | async-done | bytes 131088 | tf_op jit(solution)/shard_map/reduce_scatter | solution.py:198
  450.6 0.0 copy-done.4
  450.6 1.6 fusion.35
  (38 shorter events, 0.3 us)
Async XLA Ops:
  7.2 67.3 %copy-start = (bf16[2048,512]{1,0:T(8,128)(2,1)S(1)}, bf16[2048,512]{1,0:T(8,128)(2,1)}, u32[]{:S(2)}) copy-start(bf16[2048,512]{1,0:T(8,128)(2,1)} %param.14) | copy-start | bytes 6291460
  7.2 67.3 %all-gather.4.cloned.1.call-start = ((), (), s32[]{:S(2)}) async-start(), calls=%async_computation.3 | async-start | bytes 4325376 | tf_op jit(solution)/shard_map/all_gather | solution.py:101
  10.1 112.6 %all-gather.6.cloned.1.call-start = ((), (), s32[]{:S(2)}) async-start(), calls=%async_computation.6 | async-start | bytes 1179648 | tf_op jit(solution)/shard_map/all_gather | solution.py:125
  10.2 68.0 %copy-start.10 = (s32[1024]{0:T(1024)}, s32[1024]{0:T(1024)S(1)}, u32[]{:S(2)}) copy-start(s32[1024]{0:T(1024)S(1)} %fusion.78) | copy-start | bytes 12292
  10.3 68.0 %copy-start.7 = (bf16[2048,64]{0,1:T(8,128)(2,1)S(1)}, bf16[2048,64]{0,1:T(8,128)(2,1)}, u32[]{:S(2)}) copy-start(bf16[2048,64]{0,1:T(8,128)(2,1)} %param.13) | copy-start | bytes 786436
  78.2 5.1 %copy-start.14 = (s32[8]{0:T(128)S(1)}, s32[8]{0:T(128)}, u32[]{:S(2)}) copy-start(s32[8]{0:T(128)} %param.11) | copy-start | bytes 100
  78.2 5.7 %slice-start = ((s32[1024]{0:T(1024)}), s32[256]{0:T(256)S(1)}, s32[]{:S(2)}) async-start(s32[1024]{0:T(1024)} %copy-done.10), calls=%async_computation.7 | async-start | bytes 2048 | tf_op jit(solution)/shard_map/slice | solution.py:117
  83.3 153.8 %reduce-scatter.3.cloned.1.call-start = ((), (), s32[]{:S(2)}) async-start(), calls=%async_computation.4 | async-start | bytes 4325376 | tf_op jit(solution)/shard_map/reduce_scatter | solution.py:182
  83.3 0.5 copy-start.11
  85.4 39.5 %copy-start.6 = (bf16[8,64,64]{1,0,2:T(8,128)(2,1)}, bf16[8,64,64]{1,0,2:T(8,128)(2,1)S(1)}, u32[]{:S(2)}) copy-start(bf16[8,64,64]{1,0,2:T(8,128)(2,1)S(1)} %reshape.514) | copy-start | bytes 196612
  128.6 2.4 copy-start.1
  128.6 3.8 copy-start.5
  132.4 1.2 copy-start.8
  133.6 103.4 %copy-start.3 = (bf16[32,2048]{1,0:T(8,128)(2,1)S(1)}, bf16[32,2048]{1,0:T(8,128)(2,1)}, u32[]{:S(2)}) copy-start(bf16[32,2048]{1,0:T(8,128)(2,1)} %param.10) | copy-start | bytes 393220
  133.6 104.5 %copy-start.9 = (f32[2048]{0:T(1024)S(1)}, f32[2048]{0:T(1024)}, u32[]{:S(2)}) copy-start(f32[2048]{0:T(1024)} %param.16) | copy-start | bytes 24580
  136.9 313.7 %reduce-scatter.5.cloned.1.call-start = ((), (), s32[]{:S(2)}) async-start(), calls=%async_computation.5 | async-start | bytes 4325376 | tf_op jit(solution)/shard_map/reduce_scatter | solution.py:198
  239.6 103.1 %copy-start.13 = (bf16[2048,176]{0,1:T(8,128)(2,1)S(1)}, bf16[2048,176]{0,1:T(8,128)(2,1)}, u32[]{:S(2)}) copy-start(bf16[2048,176]{0,1:T(8,128)(2,1)} %param.17) | copy-start | bytes 2162692
  340.7 2.0 copy-start.2
  352.6 0.7 copy-start.12
  352.6 97.9 %copy-start.4 = (bf16[32,2048]{1,0:T(8,128)(2,1)S(1)}, bf16[32,2048]{1,0:T(8,128)(2,1)}, u32[]{:S(2)}) copy-start(bf16[32,2048]{1,0:T(8,128)(2,1)} %reduce-scatter.3.cloned.1.call-done) | copy-start | bytes 393220
Sparse Core Ops, SparseCore 0:
  11.1 63.2 all-gather.3
  83.4 39.3 all-gather.5
  137.0 99.9 reduce-scatter.2
  352.8 97.7 reduce-scatter.4
